TPU v7x, 256 devices: a whole 4x4x8 slice. The times are simulated.
256 devices in a mesh: row: 32 (over z, x), col: 8 (over y, core).
Axes of the slice: x: 4, y: 4, z: 8, core: 2. Of those that a mesh axis runs over, the one named last changes fastest.
Arguments:
- x_points: bfloat16 [32768, 64], P(('row', 'col')), may hold values from -6 to 6
- y_points: bfloat16 [65536, 64], P(('col', 'row')), may hold values from -6 to 6
- row_mass: bfloat16 [32768], P(('row', 'col')), may hold values from 1 to 30, as said below
- col_mass: bfloat16 [65536], P(('col', 'row')), may hold values from 1 to 30, as said below
- multipliers: bfloat16 [32768, 64], P(('row', 'col')), may hold values from -12 to 12
- col_potential: bfloat16 [65536], P(('col', 'row')), may hold values from -3 to 3
- basket: float32 [64], replicated, may hold values from 0.05 to 0.25
- damping: float32 [64], replicated, may hold values from 0.3 to 1.5
Outputs:
- row_potential: float32 [32768], P('row')
- col_potential_new: float32 [65536], P('col')
- multipliers_new: float32 [32768, 64], P(('row', 'col'))
Inputs may be any that keep to these rules, and one draw needn't show every extreme that they name: `row_mass`: weights rise along the points' order by up to a factor of three. `col_mass`: weights rise along the points' order by up to a factor of three.
All inputs are finite; a program needn't handle non-finite values.
Results may differ from a plain program's by a relative error of at most 0.0012.
Values may be sent and summed in bfloat16 or wider, within the bound.
No kernel may reach another device: no remote copies, remote signals or barrier semaphores. Data moves between devices by JAX's collectives and lax.ppermute only.
A program may use at most 64 MiB of HBM per device.

v0:
```python
import jax
import jax.numpy as jnp
from jax import lax
from jax.sharding import PartitionSpec as P

EPS = 0.5
KAPPA = 0.5
RIDGE = 1.0


def joined(value, axis, join):
    pieces = jax.tree.map(lambda part: lax.all_gather(part, axis), value)
    head = jax.tree.map(lambda part: part[0], pieces)
    tail = jax.tree.map(lambda part: part[1:], pieces)
    subtotal, _ = lax.scan(lambda subtotal, piece: (join(subtotal, piece), None), head, tail)
    return subtotal


def prepare_rows(x_rows, mult_rows, basket):
    xf = x_rows.astype(jnp.float32)
    hf = mult_rows.astype(jnp.float32)
    width = xf.shape[1]
    query = hf + 2.0 * KAPPA / width * xf
    row_term = -jnp.sum(hf * xf, axis=1) - KAPPA / width * jnp.sum(xf * xf, axis=1)
    row_basket = jnp.sum(xf * basket[None, :], axis=1)
    return (query, row_term, row_basket)


def prepare_cols(y_cols, basket):
    yf = y_cols.astype(jnp.float32)
    width = yf.shape[1]
    col_term = -(KAPPA / width) * jnp.sum(yf * yf, axis=1)
    col_basket = jnp.sum(yf * basket[None, :], axis=1)
    features = jnp.concatenate([yf, yf * yf], axis=1).astype(jnp.bfloat16)
    return (yf, col_term, col_basket, features)


def scores(query, row_term, row_basket, y_float, col_term, col_basket):
    dots = lax.dot_general(
        query,
        y_float,
        (((1,), (1,)), ((), ())),
        precision=lax.Precision.HIGHEST,
        preferred_element_type=jnp.float32,
    )
    payoff = jax.nn.relu(col_basket[None, :] - row_basket[:, None])
    return (dots + row_term[:, None] + col_term[None, :] + payoff) / EPS


def lse_join(first, second):
    top = jnp.maximum(first[0], second[0])
    total = first[1] * jnp.exp(first[0] - top) + second[1] * jnp.exp(second[0] - top)
    return (top, total)


def on_device(x_points, y_points, row_mass, col_mass, multipliers, col_potential, basket, damping):
    x_rows, mult_rows, mass_rows = (
        lax.all_gather(x_points, "col", axis=0, tiled=True),
        lax.all_gather(multipliers, "col", axis=0, tiled=True),
        lax.all_gather(row_mass, "col", axis=0, tiled=True),
    )
    y_cols, pot_cols, mass_cols = (
        lax.all_gather(y_points, "row", axis=0, tiled=True),
        lax.all_gather(col_potential, "row", axis=0, tiled=True),
        lax.all_gather(col_mass, "row", axis=0, tiled=True),
    )
    query, row_term, row_basket = prepare_rows(x_rows, mult_rows, basket)
    y_float, col_term, col_basket, features = prepare_cols(y_cols, basket)
    row_weight = mass_rows.astype(jnp.float32)
    col_weight = mass_cols.astype(jnp.float32)
    log_row = jnp.log(row_weight)
    log_col = jnp.log(col_weight)
    nrows = x_rows.shape[0]
    block = min(128, nrows)
    count = nrows // block
    starts = jnp.arange(count, dtype=jnp.int32) * block

    def cut(arr, start):
        return lax.dynamic_slice_in_dim(arr, start, block, 0)

    def block_scores(start):
        return scores(
            cut(query, start),
            cut(row_term, start),
            cut(row_basket, start),
            y_float,
            col_term,
            col_basket,
        )

    gshift = pot_cols.astype(jnp.float32) / EPS + log_col

    def row_pass(start):
        z = block_scores(start) + gshift[None, :]
        top = jnp.max(z, axis=1)
        total = jnp.sum(jnp.exp(z - top[:, None]), axis=1)
        return (top, total)

    row_tops, row_totals = lax.map(row_pass, starts)
    row_tops = row_tops.reshape(nrows)
    row_totals = row_totals.reshape(nrows)
    mu_total, nu_total = lax.psum(
        (jnp.sum(row_mass.astype(jnp.float32)), jnp.sum(col_mass.astype(jnp.float32))),
        ("row", "col"),
    )
    row_top, row_total = joined((row_tops, row_totals), "col", lse_join)
    log_nu_total = jnp.log(nu_total)
    row_potential = -EPS * (row_top + jnp.log(row_total) - log_nu_total)
    fshift = row_potential / EPS + log_row

    def col_pass(start):
        z = block_scores(start) + cut(fshift, start)[:, None]
        top = jnp.max(z, axis=0)
        total = jnp.sum(jnp.exp(z - top[None, :]), axis=0)
        return (top, total)

    col_tops, col_totals = lax.map(col_pass, starts)
    col_top = jnp.max(col_tops, axis=0)
    col_total = jnp.sum(col_totals * jnp.exp(col_tops - col_top[None, :]), axis=0)
    peak = lax.pmax(col_top, "row")
    scaled = col_total * jnp.exp(col_top - peak)
    whole = lax.psum(scaled, "row")
    col_potential_new = -EPS * (peak + jnp.log(whole) - jnp.log(mu_total))
    gq = col_potential_new / EPS + log_col - log_nu_total
    fq = row_potential / EPS

    def moment_pass(start):
        plan = jnp.exp(block_scores(start) + cut(fq, start)[:, None] + gq[None, :]).astype(
            jnp.bfloat16
        )
        both = jnp.dot(plan, features, preferred_element_type=jnp.float32)
        mass = jnp.sum(plan.astype(jnp.float32), axis=1)
        return (both, mass)

    both, mass = lax.map(moment_pass, starts)
    both = both.reshape(nrows, features.shape[1])
    mass = mass.reshape(nrows)
    share = x_points.shape[0]
    both_all, mass_all = lax.psum((both, mass), "col")
    offset = lax.axis_index("col") * share
    own_both = lax.dynamic_slice_in_dim(both_all, offset, share, 0)
    own_mass = lax.dynamic_slice_in_dim(mass_all, offset, share, 0)
    width = x_points.shape[1]
    first = own_both[:, :width]
    second = own_both[:, width:]
    xf = x_points.astype(jnp.float32)
    grad = first - xf * own_mass[:, None]
    curv = (second - 2.0 * xf * first + xf * xf * own_mass[:, None]) / EPS + RIDGE
    multipliers_new = multipliers.astype(jnp.float32) - damping[None, :] * grad / curv
    return (row_potential, col_potential_new, multipliers_new)


def solution(mesh):
    placed = (
        P(("row", "col"), None),
        P(("col", "row"), None),
        P(("row", "col")),
        P(("col", "row")),
        P(("row", "col"), None),
        P(("col", "row")),
        P(),
        P(),
    )
    return jax.shard_map(
        on_device,
        mesh=mesh,
        in_specs=placed,
        out_specs=(P("row"), P("col"), P(("row", "col"), None)),
        check_vma=False,
    )
```

profile of v0, /device:TPU:2, one launch (start us, length us, event | category | flops | bytes accessed | tf_op | source)
XLA Modules:
  0.0 851.1 jit_solution(13461661143674850518)
XLA Ops:
  7.2 1.5 copy.17
  8.8 1.3 convert_reduce_fusion.1
  10.0 1.3 convert_reduce_fusion.2
  11.3 79.4 %all-reduce = (f32[]{:T(128)}, f32[]{:T(128)}) all-reduce(f32[]{:T(128)} %convert_reduce_fusion.1, f32[]{:T(128)} %convert_reduce_fusion.2), channel_id=1, replica_groups=mesh['row'=32,'col'=8] {'row','col'}, use_global_device_ids=true, to_apply=%region_12.13 | all-reduce | flops 2 | bytes 16 | tf_op jit(solution)/shard_map/psum | solution.py:102
  93.3 0.8 copy.16
  94.2 0.8 copy.15
  95.0 42.6 %all-gather.1 = bf16[32,1,256]{2,1,0:T(2,128)(2,1)S(1)} all-gather(bf16[1,1,256]{2,1,0:T(2,128)(2,1)S(1)} %reshape.38), channel_id=1, replica_groups=mesh['row'=32,'col'=8] {'row'}, dimensions={0}, use_global_device_ids=true | all-gather | bytes 16896 | tf_op jit(solution)/shard_map/all_gather | solution.py:65
  137.6 40.5 %all-gather = bf16[32,1,256]{2,1,0:T(2,128)(2,1)S(1)} all-gather(bf16[1,1,256]{2,1,0:T(2,128)(2,1)S(1)} %reshape.36), channel_id=1, replica_groups=mesh['row'=32,'col'=8] {'row'}, dimensions={0}, use_global_device_ids=true | all-gather | bytes 16896 | tf_op jit(solution)/shard_map/all_gather | solution.py:64
  178.2 9.2 %all-gather.4 = bf16[8,1,128]{2,1,0:T(2,128)(2,1)S(1)} all-gather(bf16[1,1,128]{2,1,0:T(2,128)(2,1)} %bitcast.86), channel_id=1, replica_groups=mesh['row'=32,'col'=8] {'col'}, dimensions={0}, use_global_device_ids=true | all-gather | bytes 2304 | tf_op jit(solution)/shard_map/all_gather | solution.py:60
  187.4 12.8 %all_gather.24 = bf16[1024,64]{1,0:T(8,128)(2,1)S(1)} all-gather(bf16[128,64]{1,0:T(8,128)(2,1)S(1)} %copy.15), channel_id=1, replica_groups=mesh['row'=32,'col'=8] {'col'}, dimensions={0}, use_global_device_ids=true | all-gather | bytes 147456 | tf_op jit(solution)/shard_map/all_gather | solution.py:59
  200.2 12.8 %all_gather.25 = bf16[1024,64]{1,0:T(8,128)(2,1)S(1)} all-gather(bf16[128,64]{1,0:T(8,128)(2,1)S(1)} %copy.16), channel_id=1, replica_groups=mesh['row'=32,'col'=8] {'col'}, dimensions={0}, use_global_device_ids=true | all-gather | bytes 147456 | tf_op jit(solution)/shard_map/all_gather | solution.py:58
  213.1 1.2 fusion.24
  214.3 5.2 multiply_reduce_fusion
  219.5 2.2 convert_element_type.39
  221.7 80.0 %while.48 = (s32[]{:T(128)}, f32[8,128]{1,0:T(8,128)S(1)}, f32[8,128]{1,0:T(8,128)S(1)}, s32[8]{0:T(128)S(1)}, f32[1024,64]{1,0:T(8,128)S(1)}, /*index=5*/f32[81...) while((s32[]{:T(128)}, f32[8,128]{1,0:T(8,128)S(1)}, ...), condition=%wide.region_8.9_spmd, body=%wide.region_5.8_spmd.sunk | while | flops 815791872 | bytes 10656463 | solution.py:99
  224.4 6.5 fusion.52
  230.9 0.8 exponential_reduce_fusion.4
  234.4 6.5 fusion.52
  240.9 0.8 exponential_reduce_fusion.4
  244.4 6.5 fusion.52
  250.9 0.8 exponential_reduce_fusion.4
  254.4 6.5 fusion.52
  260.9 0.8 exponential_reduce_fusion.4
  264.4 6.5 fusion.52
  270.9 0.8 exponential_reduce_fusion.4
  274.4 6.5 fusion.52
  280.9 0.8 exponential_reduce_fusion.4
  284.4 6.5 fusion.52
  290.9 0.8 exponential_reduce_fusion.4
  294.4 6.5 fusion.52
  300.9 0.8 exponential_reduce_fusion.4
  301.7 12.9 %all-gather.2 = f32[8,1,1024]{2,1,0:T(1,128)S(1)} all-gather(f32[1,1,1024]{2,1,0:T(1,128)S(1)} %bitcast.83), channel_id=1, replica_groups=mesh['row'=32,'col'=8] {'col'}, dimensions={0}, use_global_device_ids=true | all-gather | bytes 36864 | tf_op jit(solution)/shard_map/all_gather | solution.py:12
  314.7 13.1 %all-gather.3 = f32[8,1,1024]{2,1,0:T(1,128)S(1)} all-gather(f32[1,1,1024]{2,1,0:T(1,128)S(1)} %bitcast.82), channel_id=1, replica_groups=mesh['row'=32,'col'=8] {'col'}, dimensions={0}, use_global_device_ids=true | all-gather | bytes 36864 | tf_op jit(solution)/shard_map/all_gather | solution.py:12
  328.7 80.8 %while.50 = (s32[]{:T(128)}, f32[8,8192]{1,0:T(8,128)S(1)}, f32[8,8192]{1,0:T(8,128)S(1)}, s32[8]{0:T(128)S(1)}, f32[1024,64]{1,0:T(8,128)S(1)}, /*index=5*/f32[...) while((s32[]{:T(128)}, f32[8,8192]{1,0:T(8,128)S(1)}, ...), condition=%wide.region_16.17_spmd, body=%wide.region_13.16_spmd.sunk | while | flops 815775744 | bytes 10851027 | solution.py:117
  331.5 6.4 fusion.54
  341.6 6.4 fusion.54
  351.7 6.4 fusion.54
  361.8 6.4 fusion.54
  371.9 6.4 fusion.54
  382.0 6.4 fusion.54
  392.1 6.4 fusion.54
  402.2 6.4 fusion.54
  409.7 136.0 %pmax.7 = f32[8192]{0:T(1024)S(1)} all-reduce(f32[8192]{0:T(1024)S(1)} %reduce_max.27), channel_id=1, replica_groups=mesh['row'=32,'col'=8] {'row'}, use_global_device_ids=true, to_apply=%region_18.19 | all-reduce | flops 8192 | bytes 65536 | tf_op jit(solution)/shard_map/pmax | solution.py:120
  545.8 139.9 %psum.36 = f32[8192]{0:T(1024)S(1)} all-reduce(f32[8192]{0:T(1024)S(1)} %exponential_multiply_fusion), channel_id=1, replica_groups=mesh['row'=32,'col'=8] {'row'}, use_global_device_ids=true, to_apply=%region_20.21 | all-reduce | flops 8192 | bytes 65536 | tf_op jit(solution)/shard_map/psum | solution.py:122
  686.4 3.4 pad_maximum_fusion
  689.8 88.4 %while.51 = (s32[]{:T(128)}, f32[8,128,128]{2,1,0:T(8,128)S(1)}, f32[8,128]{1,0:T(8,128)S(1)}, s32[8]{0:T(128)S(1)}, f32[1024,64]{1,0:T(8,128)S(1)}, /*index=5*/...) while((s32[]{:T(128)}, f32[8,128,128]{2,1,0:T(8,128)S(1)}, ...), condition=%wide.region_25.26_spmd, body=%wide.region_23.25_spmd.sunk | while | flops 1085276032 | bytes 8624355 | solution.py:135
  692.5 7.5 convert_reduce_fusion.4
  700.0 0.7 fusion.58
  703.6 7.5 convert_reduce_fusion.4
  711.1 0.7 fusion.58
  714.6 7.5 convert_reduce_fusion.4
  722.1 0.7 fusion.58
  725.7 7.5 convert_reduce_fusion.4
  733.2 0.7 fusion.58
  736.7 7.5 convert_reduce_fusion.4
  744.2 0.7 fusion.58
  747.8 7.5 convert_reduce_fusion.4
  758.8 7.5 convert_reduce_fusion.4
  766.3 0.7 fusion.58
  769.9 7.5 convert_reduce_fusion.4
  778.1 1.0 copy.19
  779.2 12.4 %psum.39 = f32[1024]{0:T(1024)S(1)} all-reduce(f32[1024]{0:T(1024)S(1)} %bitcast.84), channel_id=1, replica_groups=mesh['row'=32,'col'=8] {'col'}, use_global_device_ids=true, to_apply=%region_27.28 | all-reduce | flops 1024 | bytes 8192 | tf_op jit(solution)/shard_map/psum | solution.py:139
  791.7 51.1 %all-reduce.3.cloned.1.call-done = f32[1024,128]{0,1:T(8,128)} async-done(((f32[1024,128]{0,1:T(8,128)}), f32[1024,128]{0,1:T(8,128)}) %all-reduce.3.cloned.1.call-update) | async-done | bytes 524304 | tf_op jit(solution)/shard_map/psum | solution.py:139
  842.8 1.5 fusion.28
  (193 shorter events, 32.3 us)
Async XLA Ops:
  7.2 207.1 %all-gather.7.cloned.1.call-start = ((), (), s32[]{:S(2)}) async-start(), calls=%async_computation | async-start | bytes 2162688 | tf_op jit(solution)/shard_map/all_gather | solution.py:63
  8.7 834.1 %all-reduce.3.cloned.1.call-start = ((), (), s32[]{:S(2)}) async-start(), calls=%async_computation.1 | async-start | bytes 1048576 | tf_op jit(solution)/shard_map/psum | solution.py:139
  214.3 5.2 copy-start
  689.7 153.1 %copy-start.1 = (bf16[128,64]{0,1:T(8,128)(2,1)S(1)}, bf16[128,64]{0,1:T(8,128)(2,1)}, u32[]{:S(2)}) copy-start(bf16[128,64]{0,1:T(8,128)(2,1)} %param.16) | copy-start | bytes 49156
  689.7 153.1 %copy-start.2 = (bf16[128,64]{0,1:T(8,128)(2,1)S(1)}, bf16[128,64]{0,1:T(8,128)(2,1)}, u32[]{:S(2)}) copy-start(bf16[128,64]{0,1:T(8,128)(2,1)} %param.20) | copy-start | bytes 49156
  689.8 153.1 %copy-start.3 = (f32[64]{0:T(128)S(1)}, f32[64]{0:T(128)}, u32[]{:S(2)}) copy-start(f32[64]{0:T(128)} %param.23) | copy-start | bytes 772
Sparse Core Ops, SparseCore 0:
  10.6 79.5 all-gather.6
  779.3 63.4 all-reduce.2
where the time goes:
time: 853 us; the launch traced here: 851 us
  blocking collectives  512 us (60%)
  matrix products  169 us (20%)
  waiting for transfers between devices  51.2 us (6%)
  loops' own time  47.5 us (6%)
  other arithmetic  28.6 us (3%)
  local copies, waits for them, and re-layouts  27.8 us (3%)
  between operations  15.6 us (2%)
    dot_general x24, matrix products, scores(): lax.dot_general(query, y_float, (((1,), (1,)), ((), ())), precision=lax.P...  163 us
    psum x1, blocking collectives, on_device(): whole = lax.psum(scaled, 'row')  140 us
    pmax x1, blocking collectives, on_device(): peak = lax.pmax(col_top, 'row')  136 us
    psum x1, blocking collectives, on_device(): lax.psum((jnp.sum(row_mass.astype(jnp.float32)), jnp.sum(col_mass.astype(...  79.4 us
    psum x1, waiting for transfers between devices, on_device(): both_all, mass_all = lax.psum((both, mass), 'col')  51.1 us
    all_gather x1, blocking collectives, on_device(): lax.all_gather(col_mass, 'row', axis=0, tiled=True)  42.6 us
    all_gather x1, blocking collectives, on_device(): lax.all_gather(col_potential, 'row', axis=0, tiled=True)  40.5 us
    all_gather x2, blocking collectives, joined(): pieces = jax.tree.map(lambda part: lax.all_gather(part, axis), value)  26 us
  transfers between devices with their start and end apart: 2, of which 1 were waited for; matrix products, arithmetic and copies ran while one was open for 1% of the time, Pallas kernels for 0%

commit v1 on v0

--- a/solution.py
+++ b/solution.py
@@ -2,6 +2,7 @@
 import jax.numpy as jnp
 from jax import lax
 from jax.sharding import PartitionSpec as P
+from jax.lax import all_to_all, axis_size
 
 EPS = 0.5
 KAPPA = 0.5
@@ -59,9 +60,18 @@
         lax.all_gather(multipliers, "col", axis=0, tiled=True),
         lax.all_gather(row_mass, "col", axis=0, tiled=True),
     )
+    manage_boxes = lambda tile_in, mesh_dim: jnp.concatenate(
+        all_to_all(
+            jnp.stack(axis_size(mesh_dim) * [tile_in]),
+            axis_name=mesh_dim,
+            split_axis=0,
+            concat_axis=0,
+        ),
+        axis=0,
+    )
     y_cols, pot_cols, mass_cols = (
         lax.all_gather(y_points, "row", axis=0, tiled=True),
-        lax.all_gather(col_potential, "row", axis=0, tiled=True),
+        manage_boxes(col_potential, "row"),
         lax.all_gather(col_mass, "row", axis=0, tiled=True),
     )
     query, row_term, row_basket = prepare_rows(x_rows, mult_rows, basket)

time: 853 us -> 823 us (0.965)
  blocking collectives: 512 us -> 468 us
  starting transfers between devices: 0.08 us -> 11.7 us
    all_gather x1 -> x0, blocking collectives: 40.5 us -> none  [on_device(): lax.all_gather(col_potential, 'row', axis=0, tiled=True)]
    all_to_all x0 -> x1, starting transfers between devices: none -> 11.6 us  [on_device(): all_to_all(jnp.stack(axis_size(mesh_dim) * [tile_in]), axis_name=mesh_dim...]
  transfers between devices with their start and end apart: 2 -> 3, of which waited for: 1 -> 1; matrix products, arithmetic and copies ran while one was open for 1% -> 1% of each run, Pallas kernels for 0% -> 0%
where the time goes in v1:
time: 823 us; the launch traced here: 821 us
  blocking collectives  468 us (57%)
  matrix products  168 us (20%)
  waiting for transfers between devices  51.9 us (6%)
  loops' own time  47.5 us (6%)
  other arithmetic  29.3 us (4%)
  local copies, waits for them, and re-layouts  29 us (4%)
  between operations  15.6 us (2%)
  starting transfers between devices  11.7 us (1%)
    dot_general x24, matrix products, scores(): lax.dot_general(query, y_float, (((1,), (1,)), ((), ())), precision=lax.P...  163 us
    psum x1, blocking collectives, on_device(): whole = lax.psum(scaled, 'row')  140 us
    pmax x1, blocking collectives, on_device(): peak = lax.pmax(col_top, 'row')  136 us
    psum x1, blocking collectives, on_device(): lax.psum((jnp.sum(row_mass.astype(jnp.float32)), jnp.sum(col_mass.astype(...  75 us
    psum x1, waiting for transfers between devices, on_device(): both_all, mass_all = lax.psum((both, mass), 'col')  51.9 us
    all_gather x1, blocking collectives, on_device(): lax.all_gather(col_mass, 'row', axis=0, tiled=True)  42.4 us
    all_gather x2, blocking collectives, joined(): pieces = jax.tree.map(lambda part: lax.all_gather(part, axis), value)  26 us
  transfers between devices with their start and end apart: 3, of which 1 were waited for; matrix products, arithmetic and copies ran while one was open for 1% of the time, Pallas kernels for 0%

profile of v1, /device:TPU:2, one launch (start us, length us, event | category | flops | bytes accessed | tf_op | source)
XLA Modules:
  0.0 821.4 jit_solution(8236116233020089111)
XLA Ops:
  7.2 1.5 copy.17
  9.9 0.7 reduce
  11.3 11.6 %all-to-all-start = ((bf16[32,2,128]{2,1,0:T(2,128)(2,1)}), bf16[32,2,128]{2,1,0:T(2,128)(2,1)S(1)}, u32[]{:S(2)}, u32[]{:S(2)}) async-start(bf16[32,2,128]{2,1,0:T(2,128)(2,1)} %reshape.68), calls=%async_computation | async-start | bytes 32768 | tf_op jit(solution)/shard_map/all_to_all | solution.py:64
  23.6 0.8 copy.16
  24.4 0.8 copy.15
  25.3 11.0 %all-gather.3 = bf16[8,1,128]{2,1,0:T(2,128)(2,1)S(1)} all-gather(bf16[1,1,128]{2,1,0:T(2,128)(2,1)} %bitcast.86), channel_id=1, replica_groups=mesh['row'=32,'col'=8] {'col'}, dimensions={0}, use_global_device_ids=true | all-gather | bytes 2304 | tf_op jit(solution)/shard_map/all_gather | solution.py:61
  36.2 42.4 %all-gather = bf16[32,1,256]{2,1,0:T(2,128)(2,1)S(1)} all-gather(bf16[1,1,256]{2,1,0:T(2,128)(2,1)S(1)} %reshape.48), channel_id=1, replica_groups=mesh['row'=32,'col'=8] {'row'}, dimensions={0}, use_global_device_ids=true | all-gather | bytes 16896 | tf_op jit(solution)/shard_map/all_gather | solution.py:75
  78.7 12.8 %all_gather.21 = bf16[1024,64]{1,0:T(8,128)(2,1)S(1)} all-gather(bf16[128,64]{1,0:T(8,128)(2,1)S(1)} %copy.15), channel_id=1, replica_groups=mesh['row'=32,'col'=8] {'col'}, dimensions={0}, use_global_device_ids=true | all-gather | bytes 147456 | tf_op jit(solution)/shard_map/all_gather | solution.py:60
  91.5 12.8 %all_gather.22 = bf16[1024,64]{1,0:T(8,128)(2,1)S(1)} all-gather(bf16[128,64]{1,0:T(8,128)(2,1)S(1)} %copy.16), channel_id=1, replica_groups=mesh['row'=32,'col'=8] {'col'}, dimensions={0}, use_global_device_ids=true | all-gather | bytes 147456 | tf_op jit(solution)/shard_map/all_gather | solution.py:59
  104.3 1.3 convert_reduce_fusion.1
  105.6 1.3 convert_reduce_fusion.2
  106.8 1.2 fusion.24
  108.1 75.0 %all-reduce = (f32[]{:T(128)}, f32[]{:T(128)}) all-reduce(f32[]{:T(128)} %convert_reduce_fusion.1, f32[]{:T(128)} %convert_reduce_fusion.2), channel_id=1, replica_groups=mesh['row'=32,'col'=8] {'row','col'}, use_global_device_ids=true, to_apply=%region_12.13 | all-reduce | flops 2 | bytes 16 | tf_op jit(solution)/shard_map/psum | solution.py:112
  184.6 5.2 multiply_reduce_fusion
  189.8 2.2 convert_element_type.40
  192.0 79.9 %while.48 = (s32[]{:T(128)}, f32[8,128]{1,0:T(8,128)S(1)}, f32[8,128]{1,0:T(8,128)S(1)}, s32[8]{0:T(128)S(1)}, f32[1024,64]{1,0:T(8,128)S(1)}, /*index=5*/f32[81...) while((s32[]{:T(128)}, f32[8,128]{1,0:T(8,128)S(1)}, ...), condition=%wide.region_8.9_spmd, body=%wide.region_5.8_spmd.sunk | while | flops 815791872 | bytes 10656463 | solution.py:109
  194.7 6.5 fusion.52
  201.2 0.8 exponential_reduce_fusion.4
  204.7 6.5 fusion.52
  211.2 0.8 exponential_reduce_fusion.4
  214.7 6.5 fusion.52
  221.2 0.8 exponential_reduce_fusion.4
  224.7 6.5 fusion.52
  231.2 0.8 exponential_reduce_fusion.4
  234.7 6.5 fusion.52
  241.2 0.8 exponential_reduce_fusion.4
  244.7 6.5 fusion.52
  251.2 0.8 exponential_reduce_fusion.4
  254.7 6.5 fusion.52
  261.2 0.8 exponential_reduce_fusion.4
  264.7 6.5 fusion.52
  271.2 0.8 exponential_reduce_fusion.4
  272.0 12.9 %all-gather.1 = f32[8,1,1024]{2,1,0:T(1,128)S(1)} all-gather(f32[1,1,1024]{2,1,0:T(1,128)S(1)} %bitcast.83), channel_id=1, replica_groups=mesh['row'=32,'col'=8] {'col'}, dimensions={0}, use_global_device_ids=true | all-gather | bytes 36864 | tf_op jit(solution)/shard_map/all_gather | solution.py:13
  284.9 13.1 %all-gather.2 = f32[8,1,1024]{2,1,0:T(1,128)S(1)} all-gather(f32[1,1,1024]{2,1,0:T(1,128)S(1)} %bitcast.82), channel_id=1, replica_groups=mesh['row'=32,'col'=8] {'col'}, dimensions={0}, use_global_device_ids=true | all-gather | bytes 36864 | tf_op jit(solution)/shard_map/all_gather | solution.py:13
  299.0 80.8 %while.50 = (s32[]{:T(128)}, f32[8,8192]{1,0:T(8,128)S(1)}, f32[8,8192]{1,0:T(8,128)S(1)}, s32[8]{0:T(128)S(1)}, f32[1024,64]{1,0:T(8,128)S(1)}, /*index=5*/f32[...) while((s32[]{:T(128)}, f32[8,8192]{1,0:T(8,128)S(1)}, ...), condition=%wide.region_16.17_spmd, body=%wide.region_13.16_spmd.sunk | while | flops 815775744 | bytes 10851027 | solution.py:127
  301.8 6.4 fusion.54
  311.9 6.4 fusion.54
  322.0 6.4 fusion.54
  332.1 6.4 fusion.54
  342.2 6.4 fusion.54
  352.3 6.4 fusion.54
  362.4 6.4 fusion.54
  372.5 6.4 fusion.54
  379.9 135.7 %pmax.7 = f32[8192]{0:T(1024)S(1)} all-reduce(f32[8192]{0:T(1024)S(1)} %reduce_max.27), channel_id=1, replica_groups=mesh['row'=32,'col'=8] {'row'}, use_global_device_ids=true, to_apply=%region_18.19 | all-reduce | flops 8192 | bytes 65536 | tf_op jit(solution)/shard_map/pmax | solution.py:130
  515.7 139.9 %psum.36 = f32[8192]{0:T(1024)S(1)} all-reduce(f32[8192]{0:T(1024)S(1)} %exponential_multiply_fusion), channel_id=1, replica_groups=mesh['row'=32,'col'=8] {'row'}, use_global_device_ids=true, to_apply=%region_20.21 | all-reduce | flops 8192 | bytes 65536 | tf_op jit(solution)/shard_map/psum | solution.py:132
  656.3 3.4 pad_maximum_fusion
  659.7 87.9 %while.51 = (s32[]{:T(128)}, f32[8,128,128]{2,1,0:T(8,128)S(1)}, f32[8,128]{1,0:T(8,128)S(1)}, s32[8]{0:T(128)S(1)}, f32[1024,64]{1,0:T(8,128)S(1)}, /*index=5*/...) while((s32[]{:T(128)}, f32[8,128,128]{2,1,0:T(8,128)S(1)}, ...), condition=%wide.region_25.26_spmd, body=%wide.region_23.25_spmd.sunk | while | flops 1085276032 | bytes 8624355 | solution.py:145
  662.5 7.5 convert_reduce_fusion.4
  673.5 7.5 convert_reduce_fusion.4
  680.9 0.7 fusion.58
  684.5 7.5 convert_reduce_fusion.4
  691.9 0.7 fusion.58
  695.4 7.5 convert_reduce_fusion.4
  702.9 0.7 fusion.58
  706.4 7.5 convert_reduce_fusion.4
  713.9 0.7 fusion.58
  717.4 7.5 convert_reduce_fusion.4
  724.9 0.7 fusion.58
  728.4 7.5 convert_reduce_fusion.4
  739.4 7.5 convert_reduce_fusion.4
  747.6 1.0 copy.19
  748.6 12.4 %psum.39 = f32[1024]{0:T(1024)S(1)} all-reduce(f32[1024]{0:T(1024)S(1)} %bitcast.84), channel_id=1, replica_groups=mesh['row'=32,'col'=8] {'col'}, use_global_device_ids=true, to_apply=%region_27.28 | all-reduce | flops 1024 | bytes 8192 | tf_op jit(solution)/shard_map/psum | solution.py:149
  761.1 51.9 %all-reduce.3.cloned.1.call-done = f32[1024,128]{0,1:T(8,128)} async-done(((f32[1024,128]{0,1:T(8,128)}), f32[1024,128]{0,1:T(8,128)}) %all-reduce.3.cloned.1.call-update) | async-done | bytes 524304 | tf_op jit(solution)/shard_map/psum | solution.py:149
  813.0 1.5 fusion.28
  (198 shorter events, 34.1 us)
Async XLA Ops:
  7.2 177.5 %all-gather.6.cloned.1.call-start = ((), (), s32[]{:S(2)}) async-start(), calls=%async_computation.1 | async-start | bytes 2162688 | tf_op jit(solution)/shard_map/all_gather | solution.py:73
  11.3 173.3 %all-to-all-start = ((bf16[32,2,128]{2,1,0:T(2,128)(2,1)}), bf16[32,2,128]{2,1,0:T(2,128)(2,1)S(1)}, u32[]{:S(2)}, u32[]{:S(2)}) async-start(bf16[32,2,128]{2,1,0:T(2,128)(2,1)} %reshape.68), calls=%async_computation | async-start | bytes 32768 | tf_op jit(solution)/shard_map/all_to_all | solution.py:64
  22.9 790.2 %all-reduce.3.cloned.1.call-start = ((), (), s32[]{:S(2)}) async-start(), calls=%async_computation.2 | async-start | bytes 1048576 | tf_op jit(solution)/shard_map/psum | solution.py:149
  184.6 5.2 copy-start
  659.7 153.4 %copy-start.1 = (bf16[128,64]{0,1:T(8,128)(2,1)S(1)}, bf16[128,64]{0,1:T(8,128)(2,1)}, u32[]{:S(2)}) copy-start(bf16[128,64]{0,1:T(8,128)(2,1)} %param.16) | copy-start | bytes 49156
  659.7 153.4 %copy-start.2 = (bf16[128,64]{0,1:T(8,128)(2,1)S(1)}, bf16[128,64]{0,1:T(8,128)(2,1)}, u32[]{:S(2)}) copy-start(bf16[128,64]{0,1:T(8,128)(2,1)} %param.20) | copy-start | bytes 49156
  659.7 153.3 %copy-start.3 = (f32[64]{0:T(128)S(1)}, f32[64]{0:T(128)}, u32[]{:S(2)}) copy-start(f32[64]{0:T(128)} %param.23) | copy-start | bytes 772
Sparse Core Ops, SparseCore 0:
  10.6 79.6 all-gather.5
  748.8 64.2 all-reduce.2
